TPU v7x, 512 devices: a whole 4x8x8 slice. The times are simulated.
512 devices in a mesh: obs: 32 (over y, z_lo), gr: 4 (over x), gc: 4 (over z_hi, core).
Axes of the slice: x: 4, y: 8, z: 8 (z_hi: 2, z_lo: 4; z = z_hi * 4 + z_lo), core: 2. Of those that a mesh axis runs over, the one named last changes fastest.
Arguments:
- legendre: float32 [4, 256, 8192], P(None, 'obs'), may hold values from -6 to 6
- longitude: float32 [4, 256], P(None, 'obs'), may hold values from -3.140625 to 3.140625
- orders: int32 [8192], replicated, may hold values from 0 to 360, as said below
- whitening: float32 [4, 256, 256], replicated, as said below
Outputs:
- normal: float32 [16384, 16384], P('obs', ('gr', 'gc'))
Inputs may be any that keep to these rules, and one draw needn't show every extreme that they name: The orders of 8192 degree-order pairs that follow one another cyclically in the order-major ordering of a degree-360 field (order m holds degrees m to 360); the run passes from the last pair, of order 360, to the first, of order 0, so the orders rise, fall once from 360 to 0, and rise again. Each arc's whitening matrix is lower triangular with a positive diagonal.
All inputs are finite; a program needn't handle non-finite values.
Results may differ from a plain program's by a relative error of at most 0.0003.
Values sent between devices are 32-bit elements; how exact they have to be, the bound alone decides.
No kernel may reach another device: no remote copies, remote signals or barrier semaphores. Data moves between devices by JAX's collectives and lax.ppermute only.
A program may use at most 64 MiB of HBM per device.

v0:
```python
import jax
import jax.numpy as jnp
from jax import lax
from jax.sharding import PartitionSpec as P

highest = lax.Precision.HIGHEST


def trig_design(values, longitudes, order_values):
    angles = order_values * longitudes
    stacked = jnp.stack([values * jnp.cos(angles), values * jnp.sin(angles)], axis=-1)
    return stacked.reshape(values.shape[:-1] + (2 * values.shape[-1],))


def whiten(design, matrices):
    return jnp.einsum("kec,kfe->kcf", design, matrices, precision=highest)


def shards(legendre, longitude, orders, whitening):
    arcs_total, epochs_local, pairs_total = legendre.shape
    arc_length = whitening.shape[1]
    obs_count = lax.axis_size("obs")
    grid_count = lax.axis_size(("gr", "gc"))
    grid_position = lax.axis_index(("gr", "gc"))
    row_pairs = pairs_total // obs_count
    col_pairs = pairs_total // grid_count
    row_piece = row_pairs // grid_count
    order_values = orders.astype(jnp.float32)
    accumulated = jnp.zeros((2 * row_pairs, 2 * col_pairs), jnp.float32)
    for arc_index in range(arcs_total):
        values = legendre[arc_index : arc_index + 1]
        longitudes = longitude[arc_index : arc_index + 1]
        matrices = whitening[arc_index : arc_index + 1]
        batch = values.shape[0]
        col_values = lax.dynamic_slice_in_dim(values, grid_position * col_pairs, col_pairs, 2)
        col_orders = lax.dynamic_slice_in_dim(order_values, grid_position * col_pairs, col_pairs, 0)
        value_rows = lax.all_gather(col_values, "obs", axis=1, tiled=True)
        longitude_rows = lax.all_gather(longitudes, "obs", axis=1, tiled=True)
        design = trig_design(value_rows, longitude_rows[:, :, None], col_orders)
        col_panel = jnp.einsum("kec,kfe->kcf", design, matrices, precision=highest)
        grouped = values.reshape(batch, epochs_local, obs_count, grid_count, row_piece)
        row_values = lax.dynamic_index_in_dim(grouped, grid_position, 3, keepdims=False)
        row_orders = lax.dynamic_index_in_dim(
            order_values.reshape(obs_count, grid_count, row_piece), grid_position, 1, keepdims=False
        )
        outgoing = trig_design(row_values, longitudes[:, :, None, None], row_orders)
        arrived = lax.all_to_all(outgoing, "obs", split_axis=2, concat_axis=1, tiled=True)
        own_rows = whiten(arrived.reshape(batch, arc_length, 2 * row_piece), matrices)
        accumulated = accumulated + jnp.einsum(
            "kcf,kdf->cd",
            lax.all_gather(own_rows, ("gr", "gc"), axis=1, tiled=True),
            col_panel,
            precision=highest,
        )
    return accumulated


def solution(mesh):
    placed = (P(None, "obs", None), P(None, "obs"), P(), P())
    return jax.shard_map(
        shards, mesh=mesh, in_specs=placed, out_specs=P("obs", ("gr", "gc")), check_vma=False
    )
```

profile of v0, /device:TPU:1, one launch (start us, length us, event | category | flops | bytes accessed | tf_op | source)
XLA Modules:
  0.0 630.3 jit_solution(18091526618583735605)
XLA Ops:
  0.0 1.3 fusion.56
  1.3 0.7 reshape.721
  2.0 2.0 reshape.715
  4.1 1.5 constant_dynamic-slice_fusion.1
  5.5 0.7 copy.67
  6.3 0.6 slice_bitcast_fusion
  6.9 0.1 reshape.703
  7.1 0.4 copy-done.6
  7.5 0.7 reshape.709
  8.2 2.0 reshape.702
  10.2 1.5 constant_dynamic-slice_fusion.5
  12.0 2.5 fusion.50
  14.6 0.1 copy.65
  14.7 0.7 reshape.759
  15.5 13.6 %all-to-all-start.2 = ((f32[32,1,256]{2,1,0:T(1,128)}), f32[32,1,256]{2,1,0:T(1,128)}, u32[]{:S(2)}, u32[]{:S(2)}) async-start(f32[32,1,256]{2,1,0:T(1,128)} %reshape.759), calls=%async_computation.2 | async-start | bytes 65536 | tf_op jit(solution)/shard_map/all_to_all | solution.py:47
  29.1 0.8 dynamic_slice.41
  29.8 67.4 %all_gather.57 = f32[1,256,512]{2,1,0:T(8,128)S(1)} all-gather(f32[1,8,512]{2,1,0:T(8,128)S(1)} %constant_dynamic-slice_fusion), channel_id=1, replica_groups=mesh['obs'=32,'gr'=4,'gc'=4] {'obs'}, dimensions={1}, use_global_device_ids=true | all-gather | bytes 540672 | tf_op jit(solution)/shard_map/all_gather | solution.py:37
  97.3 1.3 dynamic-slice
  99.6 62.2 %all_gather.49 = f32[1,256,512]{2,1,0:T(8,128)S(1)} all-gather(f32[1,8,512]{2,1,0:T(8,128)S(1)} %constant_dynamic-slice_fusion.4), channel_id=1, replica_groups=mesh['obs'=32,'gr'=4,'gc'=4] {'obs'}, dimensions={1}, use_global_device_ids=true | all-gather | bytes 540672 | tf_op jit(solution)/shard_map/all_gather | solution.py:37
  161.8 64.1 %all_gather.53 = f32[1,256,512]{2,1,0:T(8,128)S(1)} all-gather(f32[1,8,512]{2,1,0:T(8,128)S(1)} %constant_dynamic-slice_fusion.2), channel_id=1, replica_groups=mesh['obs'=32,'gr'=4,'gc'=4] {'obs'}, dimensions={1}, use_global_device_ids=true | all-gather | bytes 540672 | tf_op jit(solution)/shard_map/all_gather | solution.py:37
  225.9 62.3 %all_gather.45 = f32[1,256,512]{2,1,0:T(8,128)S(1)} all-gather(f32[1,8,512]{2,1,0:T(8,128)S(1)} %constant_dynamic-slice_fusion.6), channel_id=1, replica_groups=mesh['obs'=32,'gr'=4,'gc'=4] {'obs'}, dimensions={1}, use_global_device_ids=true | all-gather | bytes 540672 | tf_op jit(solution)/shard_map/all_gather | solution.py:37
  288.2 62.8 %all-reduce.4 = (f32[256]{0:T(256)S(1)}, f32[256]{0:T(256)S(1)}, f32[256]{0:T(256)S(1)}, f32[256]{0:T(256)S(1)}) all-reduce(f32[256]{0:T(256)S(1)} %fusion.54, f32[256]{0:T(256)S(1)} %fusion.52, f32[256]{0:T(256)S(1)} %fusion.53, f32[256]{0:T(256)S(1)} %fusion.55), channel_id=1, replica_groups=mesh['obs'=32,'gr'=4,'gc'=4] {'obs'}, use_global_device_ids=true, to_apply=%add.2 | all-reduce | flops 1024 | bytes 8192
  351.0 8.8 %fusion.13 = (f32[1,256,512,1]{2,1,3,0:T(8,128)S(1)}, f32[1,256,512,1]{2,1,3,0:T(8,128)S(1)}, f32[1,256,512,1]{2,1,3,0:T(8,128)S(1)}, f32[1,256,512,1]{2,1,3,0:T...) fusion(f32[1,256,512]{2,1,0:T(8,128)S(1)} %all_gather.57, ...), kind=kLoop, calls=%fused_computation.26 | loop fusion | flops 1572864 | bytes 6297600 | tf_op jit(solution)/shard_map/stack | solution.py:11
  359.8 1.2 pad_maximum_fusion.2
  361.0 0.6 copy.66
  361.6 0.7 reshape.720
  362.4 0.1 copy.57
  362.6 0.7 reshape.761
  363.3 2.7 pad_maximum_fusion
  366.0 1.6 copy.58
  367.6 1.7 reshape.708
  369.3 1.0 fusion.20
  370.3 0.2 copy-done.2
  370.5 1.0 fusion.28
  371.7 0.1 copy.61
  371.8 0.7 reshape.763
  372.5 1.5 copy.62
  374.1 1.7 reshape.714
  375.8 2.3 fusion.24
  378.1 2.3 copy.70
  380.3 2.9 reshape.726
  383.2 3.3 fusion.16
  386.6 0.1 copy.69
  386.7 0.7 reshape.765
  387.5 4.3 all-to-all-start
  391.8 0.6 broadcast.450
  392.4 1.5 reduce
  393.9 1.3 fusion.22
  395.2 108.4 %all-gather.2 = f32[512,256]{1,0:T(8,128)} all-gather(f32[32,256]{1,0:T(8,128)S(1)} %fusion.22), channel_id=4, replica_groups=mesh['obs'=32,'gr'=4,'gc'=4] {'gr','gc'}, dimensions={0}, use_global_device_ids=true | all-gather | bytes 557056 | tf_op jit(solution)/shard_map/all_gather | solution.py:51
  503.6 7.2 %all-to-all-start.1 = ((f32[32,1,256]{2,1,0:T(1,128)}), f32[32,1,256]{2,1,0:T(1,128)S(1)}, u32[]{:S(2)}, u32[]{:S(2)}) async-start(f32[32,1,256]{2,1,0:T(1,128)} %reshape.763), calls=%async_computation.1 | async-start | bytes 65536 | tf_op jit(solution)/shard_map/all_to_all | solution.py:47
  510.8 0.7 reduce.1
  511.6 1.3 fusion.30
  512.9 28.4 %all-gather = f32[512,256]{1,0:T(8,128)} all-gather(f32[32,256]{1,0:T(8,128)S(1)} %fusion.30), channel_id=2, replica_groups=mesh['obs'=32,'gr'=4,'gc'=4] {'gr','gc'}, dimensions={0}, use_global_device_ids=true | all-gather | bytes 557056 | tf_op jit(solution)/shard_map/all_gather | solution.py:51
  541.3 10.0 %all-to-all-start.3 = ((f32[32,1,256]{2,1,0:T(1,128)}), f32[32,1,256]{2,1,0:T(1,128)S(1)}, u32[]{:S(2)}, u32[]{:S(2)}) async-start(f32[32,1,256]{2,1,0:T(1,128)} %reshape.765), calls=%async_computation.3 | async-start | bytes 65536 | tf_op jit(solution)/shard_map/all_to_all | solution.py:47
  551.3 0.7 reduce.2
  552.1 1.3 fusion.26
  553.4 37.7 %all-gather.1 = f32[512,256]{1,0:T(8,128)} all-gather(f32[32,256]{1,0:T(8,128)S(1)} %fusion.26), channel_id=3, replica_groups=mesh['obs'=32,'gr'=4,'gc'=4] {'gr','gc'}, dimensions={0}, use_global_device_ids=true | all-gather | bytes 557056 | tf_op jit(solution)/shard_map/all_gather | solution.py:51
  591.1 0.7 reduce.3
  591.9 1.3 fusion.18
  593.2 26.7 %all-gather.3 = f32[512,256]{1,0:T(8,128)S(1)} all-gather(f32[32,256]{1,0:T(8,128)S(1)} %fusion.18), channel_id=5, replica_groups=mesh['obs'=32,'gr'=4,'gc'=4] {'gr','gc'}, dimensions={0}, use_global_device_ids=true | all-gather | bytes 557056 | tf_op jit(solution)/shard_map/all_gather | solution.py:51
  620.0 2.9 fusion.63
  622.9 1.9 fusion.61
  624.8 1.9 fusion.62
  626.7 3.6 add_add_fusion
  (52 shorter events, 1.5 us)
Async XLA Ops:
  2.0 4.3 copy-start.8
  2.0 4.9 copy-start.7
  6.9 0.6 copy-start.6
  11.7 87.5 %copy-start.9 = (f32[4,8]{1,0:T(4,128)S(1)}, f32[4,8]{1,0:T(4,128)}, u32[]{:S(2)}) copy-start(f32[4,8]{1,0:T(4,128)} %param.5) | copy-start | bytes 388
  15.5 372.0 %all-to-all-start.2 = ((f32[32,1,256]{2,1,0:T(1,128)}), f32[32,1,256]{2,1,0:T(1,128)}, u32[]{:S(2)}, u32[]{:S(2)}) async-start(f32[32,1,256]{2,1,0:T(1,128)} %reshape.759), calls=%async_computation.2 | async-start | bytes 65536 | tf_op jit(solution)/shard_map/all_to_all | solution.py:47
  361.0 1.3 copy-start.5
  366.0 3.4 copy-start.1
  369.3 1.2 copy-start.2
  387.5 116.2 %all-to-all-start = ((f32[32,1,256]{2,1,0:T(1,128)}), f32[32,1,256]{2,1,0:T(1,128)S(1)}, u32[]{:S(2)}, u32[]{:S(2)}) async-start(f32[32,1,256]{2,1,0:T(1,128)} %reshape.761), calls=%async_computation | async-start | bytes 65536 | tf_op jit(solution)/shard_map/all_to_all | solution.py:47
  503.6 37.6 %all-to-all-start.1 = ((f32[32,1,256]{2,1,0:T(1,128)}), f32[32,1,256]{2,1,0:T(1,128)S(1)}, u32[]{:S(2)}, u32[]{:S(2)}) async-start(f32[32,1,256]{2,1,0:T(1,128)} %reshape.763), calls=%async_computation.1 | async-start | bytes 65536 | tf_op jit(solution)/shard_map/all_to_all | solution.py:47
  541.3 49.9 %all-to-all-start.3 = ((f32[32,1,256]{2,1,0:T(1,128)}), f32[32,1,256]{2,1,0:T(1,128)S(1)}, u32[]{:S(2)}, u32[]{:S(2)}) async-start(f32[32,1,256]{2,1,0:T(1,128)} %reshape.765), calls=%async_computation.3 | async-start | bytes 65536 | tf_op jit(solution)/shard_map/all_to_all | solution.py:47
  593.2 29.7 %copy-start.3 = (f32[512,256]{1,0:T(8,128)S(1)}, f32[512,256]{1,0:T(8,128)}, u32[]{:S(2)}) copy-start(f32[512,256]{1,0:T(8,128)} %all-gather) | copy-start | bytes 1572868
  622.9 1.9 copy-start.4
  624.8 1.9 copy-start
where the time goes:
time: 631 us; the launch traced here: 630 us
  blocking collectives  520 us (82%)
  starting transfers between devices  35.1 us (6%)
  local copies, waits for them, and re-layouts  32.2 us (5%)
  matrix products  23 us (4%)
  other arithmetic  18.8 us (3%)
    all_gather x4, blocking collectives, shards(): value_rows = lax.all_gather(col_values, 'obs', axis=1, tiled=True)  256 us
    all_gather x4, blocking collectives, shards(): lax.all_gather(own_rows, ('gr', 'gc'), axis=1, tiled=True)  201 us
    unnamed x1, blocking collectives  62.8 us
    all_to_all x4, starting transfers between devices, shards(): lax.all_to_all(outgoing, 'obs', split_axis=2, concat_axis=1, tiled=True)  35.1 us
    another operation x7, other arithmetic, trig_design(): jnp.stack([values * jnp.cos(angles), values * jnp.sin(angles)], axis=-1)  12.7 us
  transfers between devices with their start and end apart: 4, of which 0 were waited for; matrix products, arithmetic and copies ran while one was open for 7% of the time, Pallas kernels for 0%

commit v1 on v0

--- a/solution.py
+++ b/solution.py
@@ -34,7 +34,9 @@
         batch = values.shape[0]
         col_values = lax.dynamic_slice_in_dim(values, grid_position * col_pairs, col_pairs, 2)
         col_orders = lax.dynamic_slice_in_dim(order_values, grid_position * col_pairs, col_pairs, 0)
-        value_rows = lax.all_gather(col_values, "obs", axis=1, tiled=True)
+        value_rows = jnp.concatenate(
+            lax.all_to_all(jnp.stack([col_values] * lax.axis_size("obs")), "obs", 0, 0), axis=1
+        )
         longitude_rows = lax.all_gather(longitudes, "obs", axis=1, tiled=True)
         design = trig_design(value_rows, longitude_rows[:, :, None], col_orders)
         col_panel = jnp.einsum("kec,kfe->kcf", design, matrices, precision=highest)

time: 631 us -> 393 us (0.62)
  the two profiles are of different devices: /device:TPU:1 before, /device:TPU:33 now
where the time goes in v1:
time: 393 us; the launch traced here: 392 us
  blocking collectives  228 us (58%)
  starting transfers between devices  68.8 us (18%)
  waiting for transfers between devices  32.2 us (8%)
  local copies, waits for them, and re-layouts  27.9 us (7%)
  matrix products  18.7 us (5%)
  other arithmetic  15.4 us (4%)
    all_gather x4, blocking collectives, shards(): lax.all_gather(own_rows, ('gr', 'gc'), axis=1, tiled=True)  163 us
    unnamed x1, blocking collectives  65.6 us
    all_to_all x4, starting transfers between devices, shards(): lax.all_to_all(outgoing, 'obs', split_axis=2, concat_axis=1, tiled=True)  37.5 us
    all_to_all x4, starting transfers between devices, shards(): lax.all_to_all(jnp.stack([col_values] * lax.axis_size('obs')), 'obs', 0, 0)  31.3 us
    all_to_all x4, waiting for transfers between devices, shards(): lax.all_to_all(jnp.stack([col_values] * lax.axis_size('obs')), 'obs', 0, 0)  17 us
    all_to_all x4, waiting for transfers between devices, shards(): lax.all_to_all(outgoing, 'obs', split_axis=2, concat_axis=1, tiled=True)  15.2 us
    mul x2, other arithmetic, trig_design(): values * jnp.cos(angles)  9.87 us
    dot_general x4, matrix products, shards(): jnp.einsum('kcf,kdf->cd', lax.all_gather(own_rows, ('gr', 'gc'), axis=1,...  9.26 us
  transfers between devices with their start and end apart: 8, of which 6 were waited for; matrix products, arithmetic and copies ran while one was open for 2% of the time, Pallas kernels for 0%

profile of v1, /device:TPU:33, one launch (start us, length us, event | category | flops | bytes accessed | tf_op | source)
XLA Modules:
  0.0 392.4 jit_solution(8561155025694034372)
XLA Ops:
  0.0 1.3 fusion.48
  1.3 0.7 reshape.894
  2.2 0.7 reshape.902
  3.2 0.7 reshape.909
  4.1 0.7 reshape.916
  5.0 0.1 reshape.895
  5.3 1.0 fusion.42
  6.4 0.1 copy.57
  6.5 0.7 reshape.959
  7.3 12.2 %all-to-all-start.2 = ((f32[32,1,256]{2,1,0:T(1,128)}), f32[32,1,256]{2,1,0:T(1,128)S(1)}, u32[]{:S(2)}, u32[]{:S(2)}) async-start(f32[32,1,256]{2,1,0:T(1,128)} %reshape.959), calls=%async_computation.2 | async-start | bytes 65536 | tf_op jit(solution)/shard_map/all_to_all | solution.py:49
  19.7 0.7 reshape.957
  20.5 3.7 all-to-all-done.2
  24.2 8.3 %all-to-all-start = ((f32[32,1,256]{2,1,0:T(1,128)}), f32[32,1,256]{2,1,0:T(1,128)S(1)}, u32[]{:S(2)}, u32[]{:S(2)}) async-start(f32[32,1,256]{2,1,0:T(1,128)} %reshape.957), calls=%async_computation | async-start | bytes 65536 | tf_op jit(solution)/shard_map/all_to_all | solution.py:49
  32.7 0.7 reshape.955
  33.4 3.7 all-to-all-done
  37.1 8.4 %all-to-all-start.4 = ((f32[32,1,256]{2,1,0:T(1,128)}), f32[32,1,256]{2,1,0:T(1,128)S(1)}, u32[]{:S(2)}, u32[]{:S(2)}) async-start(f32[32,1,256]{2,1,0:T(1,128)} %reshape.955), calls=%async_computation.4 | async-start | bytes 65536 | tf_op jit(solution)/shard_map/all_to_all | solution.py:49
  45.7 0.7 reshape.961
  46.5 3.4 all-to-all-done.4
  49.9 8.6 %all-to-all-start.6 = ((f32[32,1,256]{2,1,0:T(1,128)}), f32[32,1,256]{2,1,0:T(1,128)S(1)}, u32[]{:S(2)}, u32[]{:S(2)}) async-start(f32[32,1,256]{2,1,0:T(1,128)} %reshape.961), calls=%async_computation.6 | async-start | bytes 65536 | tf_op jit(solution)/shard_map/all_to_all | solution.py:49
  58.5 4.4 %all-to-all-done.6 = f32[32,1,256]{2,1,0:T(1,128)S(1)} async-done(((f32[32,1,256]{2,1,0:T(1,128)}), f32[32,1,256]{2,1,0:T(1,128)S(1)}, u32[]{:S(2)}, u32[]{:S(2)}) %all-to-all-start.6) | async-done | bytes 32800 | tf_op jit(solution)/shard_map/all_to_all | solution.py:49
  62.9 0.9 stack.25
  63.7 8.7 %all-to-all-start.1 = ((f32[32,1,8,512]{3,2,1,0:T(8,128)}), f32[32,1,8,512]{3,2,1,0:T(8,128)S(1)}, u32[]{:S(2)}, u32[]{:S(2)}) async-start(f32[32,1,8,512]{3,2,1,0:T(8,128)} %stack.25), calls=%async_computation.1 | async-start | bytes 1048576 | tf_op jit(solution)/shard_map/all_to_all | solution.py:38
  72.5 9.6 %all-to-all-done.1 = f32[32,1,8,512]{3,2,1,0:T(8,128)S(1)} async-done(((f32[32,1,8,512]{3,2,1,0:T(8,128)}), f32[32,1,8,512]{3,2,1,0:T(8,128)S(1)}, u32[]{:S(2)}, u32[]{:S(2)}) %all-to-all-start.1) | async-done | bytes 524320 | tf_op jit(solution)/shard_map/all_to_all | solution.py:38
  82.1 0.9 stack.28
  83.0 7.9 %all-to-all-start.3 = ((f32[32,1,8,512]{3,2,1,0:T(8,128)}), f32[32,1,8,512]{3,2,1,0:T(8,128)S(1)}, u32[]{:S(2)}, u32[]{:S(2)}) async-start(f32[32,1,8,512]{3,2,1,0:T(8,128)} %stack.28), calls=%async_computation.3 | async-start | bytes 1048576 | tf_op jit(solution)/shard_map/all_to_all | solution.py:38
  91.0 1.3 dynamic-slice
  93.2 7.4 %all-to-all-done.3 = f32[32,1,8,512]{3,2,1,0:T(8,128)S(1)} async-done(((f32[32,1,8,512]{3,2,1,0:T(8,128)}), f32[32,1,8,512]{3,2,1,0:T(8,128)S(1)}, u32[]{:S(2)}, u32[]{:S(2)}) %all-to-all-start.3) | async-done | bytes 524320 | tf_op jit(solution)/shard_map/all_to_all | solution.py:38
  100.6 0.9 stack.31
  101.4 7.9 %all-to-all-start.5 = ((f32[32,1,8,512]{3,2,1,0:T(8,128)}), f32[32,1,8,512]{3,2,1,0:T(8,128)S(1)}, u32[]{:S(2)}, u32[]{:S(2)}) async-start(f32[32,1,8,512]{3,2,1,0:T(8,128)} %stack.31), calls=%async_computation.5 | async-start | bytes 1048576 | tf_op jit(solution)/shard_map/all_to_all | solution.py:38
  109.4 65.6 %all-reduce.4 = (f32[256]{0:T(256)S(1)}, f32[256]{0:T(256)S(1)}, f32[256]{0:T(256)S(1)}, f32[256]{0:T(256)S(1)}) all-reduce(f32[256]{0:T(256)S(1)} %fusion.46, f32[256]{0:T(256)S(1)} %fusion.44, f32[256]{0:T(256)S(1)} %fusion.45, f32[256]{0:T(256)S(1)} %fusion.47), channel_id=1, replica_groups=mesh['obs'=32,'gr'=4,'gc'=4] {'obs'}, use_global_device_ids=true, to_apply=%add.2 | all-reduce | flops 1024 | bytes 8192
  175.0 0.5 broadcast.534
  175.5 0.7 reduce.2
  176.3 0.7 reduce.1
  177.1 0.7 reduce
  177.9 0.7 reduce.3
  178.7 0.3 fusion.18
  179.1 0.4 fusion.22
  179.4 0.4 fusion.14
  179.8 0.9 stack.34
  180.7 6.8 %all-to-all-start.7 = ((f32[32,1,8,512]{3,2,1,0:T(8,128)}), f32[32,1,8,512]{3,2,1,0:T(8,128)S(1)}, u32[]{:S(2)}, u32[]{:S(2)}) async-start(f32[32,1,8,512]{3,2,1,0:T(8,128)} %stack.34), calls=%async_computation.7 | async-start | bytes 1048576 | tf_op jit(solution)/shard_map/all_to_all | solution.py:38
  187.5 0.3 fusion.10
  187.8 59.1 %all-gather.1 = f32[512,256]{1,0:T(8,128)} all-gather(f32[32,256]{1,0:T(8,128)S(1)} %fusion.18), channel_id=3, replica_groups=mesh['obs'=32,'gr'=4,'gc'=4] {'gr','gc'}, dimensions={0}, use_global_device_ids=true | all-gather | bytes 557056 | tf_op jit(solution)/shard_map/all_gather | solution.py:53
  246.9 36.6 %all-gather = f32[512,256]{1,0:T(8,128)} all-gather(f32[32,256]{1,0:T(8,128)S(1)} %fusion.22), channel_id=2, replica_groups=mesh['obs'=32,'gr'=4,'gc'=4] {'gr','gc'}, dimensions={0}, use_global_device_ids=true | all-gather | bytes 557056 | tf_op jit(solution)/shard_map/all_gather | solution.py:53
  283.5 28.2 %all-gather.2 = f32[512,256]{1,0:T(8,128)} all-gather(f32[32,256]{1,0:T(8,128)S(1)} %fusion.14), channel_id=4, replica_groups=mesh['obs'=32,'gr'=4,'gc'=4] {'gr','gc'}, dimensions={0}, use_global_device_ids=true | all-gather | bytes 557056 | tf_op jit(solution)/shard_map/all_gather | solution.py:53
  311.7 38.8 %all-gather.3 = f32[512,256]{1,0:T(8,128)} all-gather(f32[32,256]{1,0:T(8,128)S(1)} %fusion.10), channel_id=5, replica_groups=mesh['obs'=32,'gr'=4,'gc'=4] {'gr','gc'}, dimensions={0}, use_global_device_ids=true | all-gather | bytes 557056 | tf_op jit(solution)/shard_map/all_gather | solution.py:53
  350.5 8.9 %fusion.6 = (f32[1,256,512,1]{2,1,3,0:T(8,128)}, f32[1,256,512,1]{2,1,3,0:T(8,128)}, f32[1,256,512,1]{2,1,3,0:T(8,128)S(1)}, f32[1,256,512,1]{2,1,3,0:T(8,128)S(...) fusion(f32[32,1,8,512]{3,2,1,0:T(8,128)S(1)} %all-to-all-done.7, ...), kind=kLoop, calls=%fused_computation.19 | loop fusion | flops 1572864 | bytes 6297600 | tf_op jit(solution)/shard_map/mul | solution.py:11
  359.3 1.1 pad_maximum_fusion
  360.5 0.6 copy.58
  361.0 0.7 reshape.908
  361.8 1.0 fusion.16
  362.8 1.5 copy.54
  364.3 1.7 reshape.901
  366.0 2.4 fusion.20
  368.5 1.5 pad_maximum_fusion.2
  370.0 1.5 copy.62
  371.5 1.7 reshape.915
  373.2 2.3 fusion.12
  375.5 2.3 copy.66
  377.8 2.9 reshape.922
  380.7 2.4 fusion.8
  383.1 1.9 fusion.54
  385.0 1.9 fusion.53
  386.9 1.9 fusion.55
  388.8 3.6 add_add_fusion
  (62 shorter events, 2.5 us)
Async XLA Ops:
  0.0 1.3 copy-start.9
  3.9 1.4 copy-start.10
  7.3 16.9 %all-to-all-start.2 = ((f32[32,1,256]{2,1,0:T(1,128)}), f32[32,1,256]{2,1,0:T(1,128)S(1)}, u32[]{:S(2)}, u32[]{:S(2)}) async-start(f32[32,1,256]{2,1,0:T(1,128)} %reshape.959), calls=%async_computation.2 | async-start | bytes 65536 | tf_op jit(solution)/shard_map/all_to_all | solution.py:49
  24.2 12.9 %all-to-all-start = ((f32[32,1,256]{2,1,0:T(1,128)}), f32[32,1,256]{2,1,0:T(1,128)S(1)}, u32[]{:S(2)}, u32[]{:S(2)}) async-start(f32[32,1,256]{2,1,0:T(1,128)} %reshape.957), calls=%async_computation | async-start | bytes 65536 | tf_op jit(solution)/shard_map/all_to_all | solution.py:49
  37.1 12.8 %all-to-all-start.4 = ((f32[32,1,256]{2,1,0:T(1,128)}), f32[32,1,256]{2,1,0:T(1,128)S(1)}, u32[]{:S(2)}, u32[]{:S(2)}) async-start(f32[32,1,256]{2,1,0:T(1,128)} %reshape.955), calls=%async_computation.4 | async-start | bytes 65536 | tf_op jit(solution)/shard_map/all_to_all | solution.py:49
  49.9 13.0 %all-to-all-start.6 = ((f32[32,1,256]{2,1,0:T(1,128)}), f32[32,1,256]{2,1,0:T(1,128)S(1)}, u32[]{:S(2)}, u32[]{:S(2)}) async-start(f32[32,1,256]{2,1,0:T(1,128)} %reshape.961), calls=%async_computation.6 | async-start | bytes 65536 | tf_op jit(solution)/shard_map/all_to_all | solution.py:49
  63.7 18.4 %all-to-all-start.1 = ((f32[32,1,8,512]{3,2,1,0:T(8,128)}), f32[32,1,8,512]{3,2,1,0:T(8,128)S(1)}, u32[]{:S(2)}, u32[]{:S(2)}) async-start(f32[32,1,8,512]{3,2,1,0:T(8,128)} %stack.25), calls=%async_computation.1 | async-start | bytes 1048576 | tf_op jit(solution)/shard_map/all_to_all | solution.py:38
  72.5 106.2 %copy-start = (f32[4,256,256]{2,1,0:T(8,128)S(1)}, f32[4,256,256]{2,1,0:T(8,128)}, u32[]{:S(2)}) copy-start(f32[4,256,256]{2,1,0:T(8,128)} %param.7) | copy-start | bytes 3145732
  83.0 17.6 %all-to-all-start.3 = ((f32[32,1,8,512]{3,2,1,0:T(8,128)}), f32[32,1,8,512]{3,2,1,0:T(8,128)S(1)}, u32[]{:S(2)}, u32[]{:S(2)}) async-start(f32[32,1,8,512]{3,2,1,0:T(8,128)} %stack.28), calls=%async_computation.3 | async-start | bytes 1048576 | tf_op jit(solution)/shard_map/all_to_all | solution.py:38
  101.4 78.4 %all-to-all-start.5 = ((f32[32,1,8,512]{3,2,1,0:T(8,128)}), f32[32,1,8,512]{3,2,1,0:T(8,128)S(1)}, u32[]{:S(2)}, u32[]{:S(2)}) async-start(f32[32,1,8,512]{3,2,1,0:T(8,128)} %stack.31), calls=%async_computation.5 | async-start | bytes 1048576 | tf_op jit(solution)/shard_map/all_to_all | solution.py:38
  180.7 169.8 %all-to-all-start.7 = ((f32[32,1,8,512]{3,2,1,0:T(8,128)}), f32[32,1,8,512]{3,2,1,0:T(8,128)S(1)}, u32[]{:S(2)}, u32[]{:S(2)}) async-start(f32[32,1,8,512]{3,2,1,0:T(8,128)} %stack.34), calls=%async_computation.7 | async-start | bytes 1048576 | tf_op jit(solution)/shard_map/all_to_all | solution.py:38
  366.0 2.4 copy-start.5
  366.0 2.4 copy-start.6
  366.0 2.4 copy-start.7
  366.0 2.4 copy-start.8
  380.7 2.4 copy-start.4
  383.1 1.9 copy-start.3
  385.0 1.9 copy-start.2
  386.9 1.9 copy-start.1
